TPU v7x, 32 devices: a whole 2x2x4 slice. The times are simulated.
32 devices in a mesh: dp: 4 (over x, core), cent: 4 (over z), rep: 2 (over y).
Axes of the slice: x: 2, y: 2, z: 4, core: 2. Of those that a mesh axis runs over, the one named last changes fastest.
Arguments:
- points: bfloat16 [4096, 1024], P('dp'), may hold values from -6 to 6
- centroids: bfloat16 [8, 2048, 1024], P('rep', 'cent'), may hold values from -1.5 to 1.5
- counts: int32 [8, 4096], P('rep', 'dp'), may hold values from 0 to 5, as said below
Outputs:
- updated: bfloat16 [8, 2048, 1024], P('rep', 'cent', 'dp')
- bagged_score: float32 [4096], P('dp')
Inputs may be any that keep to these rules, and one draw needn't show every extreme that they name: `counts`: in every replicate some point has count 5.
All inputs are finite; a program needn't handle non-finite values.
Results may differ from a plain program's by a relative error of at most 0.0045.
Values sent between devices are 32-bit elements; how exact they have to be, the bound alone decides.
No kernel may reach another device: no remote copies, remote signals or barrier semaphores. Data moves between devices by JAX's collectives and lax.ppermute only.
A program may use at most 64 MiB of HBM per device.

v0:
```python
import math

import jax
import jax.numpy as jnp
from jax import lax
from jax.sharding import PartitionSpec as P

prior_weight = 1.0


def shards(points, centroids, counts):
    rep_local, cent_local, features = centroids.shape
    squares = jnp.sum(jnp.square(centroids.astype(jnp.float32)), axis=2)
    logits = (
        jnp.einsum("nd,rkd->rnk", points, centroids, preferred_element_type=jnp.float32)
        - 0.5 * squares[:, None, :]
    )
    row_top = lax.pmax(jnp.max(logits, axis=2), "cent")
    row_total = lax.psum(jnp.sum(jnp.exp(logits - row_top[:, :, None]), axis=2), "cent")
    weights = counts.astype(jnp.float32)
    weighted = (
        jnp.exp(logits - row_top[:, :, None]) / row_total[:, :, None] * weights[:, :, None]
    ).astype(jnp.bfloat16)
    cluster_mass = lax.psum(jnp.sum(weighted.astype(jnp.float32), axis=1), "dp")
    slab_width = features // lax.axis_size("dp")
    position = lax.axis_index("dp")
    moment_sums = jnp.einsum("rnk,nd->rkd", weighted, points, preferred_element_type=jnp.float32)
    moments = lax.psum_scatter(moment_sums, "dp", scatter_dimension=2, tiled=True)
    own_slice = lax.dynamic_slice_in_dim(centroids, position * slab_width, slab_width, 2).astype(
        jnp.float32
    )
    updated = (
        (moments + prior_weight * own_slice) / (cluster_mass[:, :, None] + prior_weight)
    ).astype(jnp.bfloat16)
    log_total = row_top + jnp.log(row_total)
    summed = lax.psum(jnp.sum(log_total, axis=0), "rep")
    replicas = rep_local * lax.axis_size("rep")
    clusters = cent_local * lax.axis_size("cent")
    bagged_score = summed / replicas - math.log(clusters)
    return (updated, bagged_score)


def solution(mesh):
    return jax.shard_map(
        shards,
        mesh=mesh,
        in_specs=(P("dp", None), P("rep", "cent", None), P("rep", "dp")),
        out_specs=(P("rep", "cent", "dp"), P("dp")),
        check_vma=False,
    )
```

profile of v0, /device:TPU:0, one launch (start us, length us, event | category | flops | bytes accessed | tf_op | source)
XLA Modules:
  0.0 151.3 jit_solution(5146502373833859516)
XLA Ops:
  7.2 0.0 copy-start
  7.2 0.0 reduce-scatter.2.cloned.1.call-start
  7.2 3.2 %multiply_reduce_fusion = f32[4,512]{1,0:T(4,128)S(1)} fusion(bf16[4,512,1024]{2,1,0:T(8,128)(2,1)} %param.4), kind=kLoop, calls=%fused_computation.5 | loop fusion | flops 6289408 | bytes 4202496 | tf_op jit(solution)/shard_map/reduce_sum | solution.py:13
  10.5 0.0 copy-done
  10.5 9.1 %bitcast_reduce_fusion = (f32[4,1024]{1,0:T(4,128)S(1)}, f32[4,512,1024]{2,1,0:T(8,128)}) fusion(f32[4,512]{1,0:T(4,128)S(1)} %broadcast_multiply_fusion, bf16[4,512,1024]{2,1,0:T(8,128)(2,1)} %param.4, bf16[1024,1024]{1,0:T(8,128)(2,1)S(1)} %copy-done), kind=kOutput, calls=%fused_computation.1 | convolution fusion | flops 4299157504 | bytes 14704640 | tf_op jit(solution)/shard_map/nd,rkd->rnk/dot_general | solution.py:15
  19.5 0.0 copy-start.1
  19.5 20.6 %pmax.7 = f32[4,1024]{1,0:T(4,128)S(1)} all-reduce(f32[4,1024]{1,0:T(4,128)S(1)} %get-tuple-element.4), channel_id=1, replica_groups=mesh['dp'=4,'cent'=4,'rep'=2] {'cent'}, use_global_device_ids=true, to_apply=%region_2.0 | all-reduce | flops 4096 | bytes 32768 | tf_op jit(solution)/shard_map/pmax | solution.py:18
  40.2 4.2 %fusion.1 = f32[4,1024]{1,0:T(4,128)S(1)} fusion(f32[4,512,1024]{2,1,0:T(8,128)} %get-tuple-element.5, f32[4,1024]{1,0:T(4,128)S(1)} %pmax.7, f32[4,512]{1,0:T(4,128)S(1)} %broadcast_multiply_fusion), kind=kLoop, calls=%fused_computation.6 | loop fusion | flops 6287360 | bytes 8429568 | tf_op jit(solution)/shard_map/reduce_sum | solution.py:19
  44.4 15.5 %psum.21 = f32[4,1024]{1,0:T(4,128)S(1)} all-reduce(f32[4,1024]{1,0:T(4,128)S(1)} %fusion.1), channel_id=1, replica_groups=mesh['dp'=4,'cent'=4,'rep'=2] {'cent'}, use_global_device_ids=true, to_apply=%region_4.0 | all-reduce | flops 4096 | bytes 32768 | tf_op jit(solution)/shard_map/psum | solution.py:19
  60.0 0.0 copy-done.1
  60.0 4.8 %convert_reduce_fusion = (f32[4,512]{1,0:T(4,128)S(1)}, bf16[4,1024,512]{1,2,0:T(8,128)(2,1)S(1)}) fusion(f32[4,1024]{1,0:T(4,128)S(1)} %convert_element_type.19, f32[4,1024]{1,0:T(4,128)S(1)} %psum.21, f32[4,1024]{1,0:T(4,128)S(1)} %pmax.7, f32[4,512,1024]{2,1,0:T(8,128)} %get-tuple-element.5, f32[4,512]{1,0:T(4,128)S(1)} %broadcast_multiply_fusion), kind=kLoop, calls=%fused_computation.3 | loop fusion | flops 14678016 | bytes 12648448 | tf_op jit(solution)/shard_map/reduce_sum | solution.py:24
  64.7 6.6 %fusion.2 = f32[4,512,1024]{2,1,0:T(8,128)} fusion(bf16[4,1024,512]{1,2,0:T(8,128)(2,1)S(1)} %get-tuple-element.3, bf16[1024,1024]{1,0:T(8,128)(2,1)S(1)} %copy-done), kind=kOutput, calls=%fused_computation.7 | convolution fusion | flops 4294967296 | bytes 14680064 | tf_op jit(solution)/shard_map/rnk,nd->rkd/dot_general | solution.py:27
  71.4 0.0 reduce-scatter.2.cloned.1.call-update
  71.4 4.9 %psum.23 = f32[1024]{0:T(1024)S(1)} all-reduce(f32[1024]{0:T(1024)S(1)} %add_reduce_fusion), channel_id=1, replica_groups=mesh['dp'=4,'cent'=4,'rep'=2] {'rep'}, use_global_device_ids=true, to_apply=%region_9.0 | all-reduce | flops 1024 | bytes 8192 | tf_op jit(solution)/shard_map/psum | solution.py:36
  76.4 5.7 %psum.22 = f32[4,512]{1,0:T(4,128)S(1)} all-reduce(f32[4,512]{1,0:T(4,128)S(1)} %get-tuple-element.2), channel_id=1, replica_groups=mesh['dp'=4,'cent'=4,'rep'=2] {'dp'}, use_global_device_ids=true, to_apply=%region_7.0 | all-reduce | flops 2048 | bytes 16384 | tf_op jit(solution)/shard_map/psum | solution.py:24
  82.1 0.6 multiply_add_fusion
  82.7 58.6 %reduce-scatter.2.cloned.1.call-done = f32[4,512,256]{2,1,0:T(8,128)} async-done(((f32[4,512,1024]{2,1,0:T(8,128)}), f32[4,512,256]{2,1,0:T(8,128)}) %reduce-scatter.2.cloned.1.call-update) | async-done | bytes 2097168 | tf_op jit(solution)/shard_map/reduce_scatter | solution.py:28
  141.3 3.2 %divide_convert_fusion = bf16[4,512,256]{2,1,0:T(8,128)(2,1)} fusion(f32[4,512,256]{2,1,0:T(8,128)} %reduce-scatter.2.cloned.1.call-done, f32[4,512]{1,0:T(4,128)S(1)} %broadcast_add_fusion, bf16[4,512,1024]{2,1,0:T(8,128)(2,1)} %param.4, s32[]{:T(128)S(6)} %select_n.3), kind=kLoop, calls=%fused_computation.11 | loop fusion | flops 2097152 | bytes 4202500 | tf_op jit(solution)/shard_map/convert_element_type | solution.py:34
  (4 shorter events, 0.0 us)
Async XLA Ops:
  7.2 3.3 %copy-start = (bf16[1024,1024]{1,0:T(8,128)(2,1)S(1)}, bf16[1024,1024]{1,0:T(8,128)(2,1)}, u32[]{:S(2)}) copy-start(bf16[1024,1024]{1,0:T(8,128)(2,1)} %param.3) | copy-start | bytes 6291460
  7.2 134.2 %reduce-scatter.2.cloned.1.call-start = ((), (), s32[]{:S(2)}) async-start(), calls=%async_computation.1 | async-start | bytes 10485760 | tf_op jit(solution)/shard_map/reduce_scatter | solution.py:28
  19.5 40.4 %copy-start.1 = (s32[4,1024]{1,0:T(4,128)S(1)}, s32[4,1024]{1,0:T(4,128)}, u32[]{:S(2)}) copy-start(s32[4,1024]{1,0:T(4,128)} %param.5) | copy-start | bytes 49156
Sparse Core Ops, SparseCore 0:
  71.5 69.7 reduce-scatter.1
where the time goes:
time: 152 us; the launch traced here: 151 us
  waiting for transfers between devices  58.6 us (39%)
  blocking collectives  46.8 us (31%)
  other arithmetic  16 us (11%)
  matrix products  15.7 us (10%)
  between operations  14.1 us (9%)
    reduce_scatter x1, waiting for transfers between devices, shards(): lax.psum_scatter(moment_sums, 'dp', scatter_dimension=2, tiled=True)  58.6 us
    pmax x1, blocking collectives, shards(): row_top = lax.pmax(jnp.max(logits, axis=2), 'cent')  20.6 us
    psum x1, blocking collectives, shards(): lax.psum(jnp.sum(jnp.exp(logits - row_top[:, :, None]), axis=2), 'cent')  15.5 us
    dot_general x1, matrix products, shards(): jnp.einsum('nd,rkd->rnk', points, centroids, preferred_element_type=jnp.f...  9.08 us
    dot_general x1, matrix products, shards(): jnp.einsum('rnk,nd->rkd', weighted, points, preferred_element_type=jnp.fl...  6.64 us
    psum x1, blocking collectives, shards(): cluster_mass = lax.psum(jnp.sum(weighted.astype(jnp.float32), axis=1), 'dp')  5.74 us
    psum x1, blocking collectives, shards(): summed = lax.psum(jnp.sum(log_total, axis=0), 'rep')  4.94 us
    reduce_sum x1, other arithmetic, shards(): cluster_mass = lax.psum(jnp.sum(weighted.astype(jnp.float32), axis=1), 'dp')  4.77 us
  transfers between devices with their start and end apart: 1, of which 1 were waited for; matrix products, arithmetic and copies ran while one was open for 0% of the time, Pallas kernels for 0%

commit v1 on v0

v1 whole, which is shorter than its diff:
```python
import math

import jax
import jax.numpy as jnp
from jax import lax
from jax.sharding import PartitionSpec as P

prior_weight = 1.0


def _all_gather_shifts(x, axis):
    n = lax.axis_size(axis)
    outs = [x]
    for s in range(1, n):
        outs.append(lax.ppermute(x, axis, [(i, (i + s) % n) for i in range(n)]))
    return jnp.stack(outs)


def _all_reduce_doubling(x, axis):
    n = lax.axis_size(axis)
    if n & (n - 1):
        return lax.psum(x, axis)
    b = 1
    while b < n:
        x = x + lax.ppermute(x, axis, [(i, i ^ b) for i in range(n)])
        b *= 2
    return x


def _reduce_scatter_halving(pieces, axis):
    n = lax.axis_size(axis)
    index = lax.axis_index(axis)
    b = 1
    while b < n:
        m = pieces.shape[0] // 2
        view = pieces.reshape((m, 2) + pieces.shape[1:])
        mine = (index // b) % 2
        keep = lax.dynamic_index_in_dim(view, mine, axis=1, keepdims=False)
        send = lax.dynamic_index_in_dim(view, 1 - mine, axis=1, keepdims=False)
        pieces = keep + lax.ppermute(send, axis, [(i, i ^ b) for i in range(n)])
        b *= 2
    return pieces[0]


def shards(points, centroids, counts):
    rep_local, cent_local, features = centroids.shape
    ndp = lax.axis_size("dp")
    slab_width = features // ndp
    position = lax.axis_index("dp")
    points3 = points.reshape(points.shape[0], ndp, slab_width)
    updated = []
    log_total = []
    for r in range(rep_local):
        center = centroids[r]
        squares = jnp.sum(jnp.square(center.astype(jnp.float32)), axis=1)
        logits = (
            jnp.dot(points, center.T, preferred_element_type=jnp.float32) - 0.5 * squares[None, :]
        )
        local_top = jnp.max(logits, axis=1)
        local_total = jnp.sum(jnp.exp(logits - local_top[:, None]), axis=1)
        gathered = _all_gather_shifts(jnp.stack([local_top, local_total]), "cent")
        row_top = jnp.max(gathered[:, 0], axis=0)
        row_total = jnp.sum(gathered[:, 1] * jnp.exp(gathered[:, 0] - row_top[None, :]), axis=0)
        weights = counts[r].astype(jnp.float32)
        weighted = (
            jnp.exp(logits - row_top[:, None]) / row_total[:, None] * weights[:, None]
        ).astype(jnp.bfloat16)
        mass = _all_reduce_doubling(jnp.sum(weighted.astype(jnp.float32), axis=0), "dp")
        pieces = jnp.einsum("nk,njd->jkd", weighted, points3, preferred_element_type=jnp.float32)
        moments = _reduce_scatter_halving(pieces, "dp")
        own_slice = lax.dynamic_slice_in_dim(center, position * slab_width, slab_width, 1).astype(
            jnp.float32
        )
        updated.append(
            ((moments + prior_weight * own_slice) / (mass[:, None] + prior_weight)).astype(
                jnp.bfloat16
            )
        )
        log_total.append(row_top + jnp.log(row_total))
    updated = jnp.stack(updated)
    summed = _all_reduce_doubling(sum(log_total), "rep")
    replicas = rep_local * lax.axis_size("rep")
    clusters = cent_local * lax.axis_size("cent")
    bagged_score = summed / replicas - math.log(clusters)
    return (updated, bagged_score)


def solution(mesh):
    return jax.shard_map(
        shards,
        mesh=mesh,
        in_specs=(P("dp", None), P("rep", "cent", None), P("rep", "dp")),
        out_specs=(P("rep", "cent", "dp"), P("dp")),
        check_vma=False,
    )
```

time: 152 us -> 112 us (0.74)
  blocking collectives: 46.8 us -> 0 us
  starting transfers between devices: 0.04 us -> 32.5 us
  waiting for transfers between devices: 58.6 us -> 45.4 us
  between operations: 14.1 us -> 1.35 us
  local copies, waits for them, and re-layouts: 0.01 us -> 4.75 us
  matrix products: 15.7 us -> 11.8 us
    reduce_scatter x1 -> x0, waiting for transfers between devices: 58.6 us -> none  [shards(): lax.psum_scatter(moment_sums, 'dp', scatter_dimension=2, tiled=True)]
    ppermute x0 -> x29, waiting for transfers between devices: none -> 45.4 us  [the longest x8 34.1 us: _reduce_scatter_halving(): pieces = keep + lax.ppermute(send, axis, [(i, i ^ b) for i in range(n)])]
    ppermute x0 -> x29, starting transfers between devices: none -> 32.5 us  [the longest x12 18.8 us: _all_gather_shifts(): outs.append(lax.ppermute(x, axis, [(i, (i + s) % n) for i in range(n)]))]
    psum x3 -> x0, blocking collectives: 26.2 us -> none  [the longest x1 15.5 us: shards(): lax.psum(jnp.sum(jnp.exp(logits - row_top[:, :, None]), axis=2), 'cent')]
    pmax x1 -> x0, blocking collectives: 20.6 us -> none  [shards(): row_top = lax.pmax(jnp.max(logits, axis=2), 'cent')]
    dot_general x2 -> x8, matrix products: 15.7 us -> 11.8 us  [the longest x4 6.76 us: shards(): jnp.dot(points, center.T, preferred_element_type=jnp.float32)]
    reduce_sum x4 -> x13, other arithmetic: 12.2 us -> 9.52 us  [the longest x4 4.52 us: shards(): jnp.sum(weighted.astype(jnp.float32), axis=0)]
    unnamed x4 -> x18, local copies, waits for them, and re-layouts: 0.01 us -> 2.4 us
  transfers between devices with their start and end apart: 1 -> 29, of which waited for: 1 -> 11; matrix products, arithmetic and copies ran while one was open for 0% -> 20% of each run, Pallas kernels for 0% -> 0%
where the time goes in v1:
time: 112 us; the launch traced here: 111 us
  waiting for transfers between devices  45.4 us (41%)
  starting transfers between devices  32.5 us (29%)
  other arithmetic  15.6 us (14%)
  matrix products  11.8 us (11%)
  local copies, waits for them, and re-layouts  4.75 us (4%)
  between operations  1.35 us (1%)
    ppermute x8, waiting for transfers between devices, _reduce_scatter_halving(): pieces = keep + lax.ppermute(send, axis, [(i, i ^ b) for i in range(n)])  34.1 us
    ppermute x12, starting transfers between devices, _all_gather_shifts(): outs.append(lax.ppermute(x, axis, [(i, (i + s) % n) for i in range(n)]))  18.8 us
    ppermute x9, waiting for transfers between devices, _all_reduce_doubling(): x = x + lax.ppermute(x, axis, [(i, i ^ b) for i in range(n)])  8.69 us
    ppermute x9, starting transfers between devices, _all_reduce_doubling(): x = x + lax.ppermute(x, axis, [(i, i ^ b) for i in range(n)])  8.32 us
    dot_general x4, matrix products, shards(): jnp.dot(points, center.T, preferred_element_type=jnp.float32)  6.76 us
    ppermute x8, starting transfers between devices, _reduce_scatter_halving(): pieces = keep + lax.ppermute(send, axis, [(i, i ^ b) for i in range(n)])  5.4 us
    dot_general x4, matrix products, shards(): jnp.einsum('nk,njd->jkd', weighted, points3, preferred_element_type=jnp.f...  5.07 us
    reduce_sum x4, other arithmetic, shards(): jnp.sum(weighted.astype(jnp.float32), axis=0)  4.52 us
  transfers between devices with their start and end apart: 29, of which 11 were waited for; matrix products, arithmetic and copies ran while one was open for 20% of the time, Pallas kernels for 0%

profile of v1, /device:TPU:0, one launch (start us, length us, event | category | flops | bytes accessed | tf_op | source)
XLA Modules:
  0.0 111.4 jit_solution(2964673736609780337)
XLA Ops:
  0.6 3.2 %multiply_reduce_fusion.3 = (f32[512]{0:T(512)S(1)}, f32[512]{0:T(512)S(1)}, f32[512]{0:T(512)S(1)}, f32[512]{0:T(512)S(1)}) fusion(bf16[4,512,1024]{2,1,0:T(8,128)(2,1)} %param.4), kind=kLoop, calls=%fused_computation.23 | loop fusion | flops 6289408 | bytes 4202496 | tf_op jit(solution)/shard_map/reduce_sum | solution.py:55
  4.1 2.9 %subtract_reduce_fusion = (f32[1024]{0:T(1024)S(1)}, f32[1024,512]{0,1:T(8,128)S(1)}) fusion(f32[512]{0:T(512)S(1)} %get-tuple-element.38, bf16[1024,1024]{1,0:T(8,128)(2,1)} %param.3, bf16[4,512,1024]{2,1,0:T(8,128)(2,1)S(1)} %copy-done), kind=kOutput, calls=%fused_computation.24 | convolution fusion | flops 1074789376 | bytes 5249024 | tf_op jit(solution)/shard_map/dot_general | solution.py:57
  7.4 5.1 %collective-permute-start.23 = (f32[2,1024]{1,0:T(2,128)S(1)}, f32[2,1024]{1,0:T(2,128)S(1)}, u32[]{:S(2)}, u32[]{:S(2)}) collective-permute-start(f32[2,1024]{1,0:T(2,128)S(1)} %get-tuple-element.29), channel_id=1, source_target_pairs={{0,6},{2,0},{4,2},{6,4},{1,7},{3,1},{5,3},{7,5},{8,14},{10,8},{12,... | collective-permute-start | bytes 24584 | tf_op jit(solution)/shard_map/ppermute | solution.py:15
  16.7 2.9 %collective-permute-start.16 = (f32[2,1024]{1,0:T(2,128)S(1)}, f32[2,1024]{1,0:T(2,128)S(1)}, u32[]{:S(2)}, u32[]{:S(2)}) collective-permute-start(f32[2,1024]{1,0:T(2,128)S(1)} %get-tuple-element.27), channel_id=1, source_target_pairs={{0,6},{2,0},{4,2},{6,4},{1,7},{3,1},{5,3},{7,5},{8,14},{10,8},{12,... | collective-permute-start | bytes 24584 | tf_op jit(solution)/shard_map/ppermute | solution.py:15
  20.6 1.7 %fusion.44 = (bf16[1,512,1024]{2,1,0:T(8,128)(2,1)S(1)}, bf16[1,512,1024]{2,1,0:T(8,128)(2,1)}, bf16[1,512,1024]{2,1,0:T(8,128)(2,1)}, bf16[1,512,1024]{2,1,0:T(8,128)(2,1)}) fusion(bf16[4,512,1024]{2,1,0:T(8,128)(2,1)S(1)} %copy-done), kind=kLoop, calls=%fused_computation.115 | loop fusion | bytes 8388608 | tf_op jit(solution)/shard_map/slice | solution.py:54
  26.2 3.9 %collective-permute-start.9 = (f32[2,1024]{1,0:T(2,128)S(1)}, f32[2,1024]{1,0:T(2,128)S(1)}, u32[]{:S(2)}, u32[]{:S(2)}) collective-permute-start(f32[2,1024]{1,0:T(2,128)S(1)} %get-tuple-element.25), channel_id=1, source_target_pairs={{0,6},{2,0},{4,2},{6,4},{1,7},{3,1},{5,3},{7,5},{8,14},{10,8},{12,... | collective-permute-start | bytes 24584 | tf_op jit(solution)/shard_map/ppermute | solution.py:15
  31.6 2.8 %collective-permute-start.2 = (f32[2,1024]{1,0:T(2,128)S(1)}, f32[2,1024]{1,0:T(2,128)S(1)}, u32[]{:S(2)}, u32[]{:S(2)}) collective-permute-start(f32[2,1024]{1,0:T(2,128)S(1)} %get-tuple-element.23), channel_id=1, source_target_pairs={{0,6},{2,0},{4,2},{6,4},{1,7},{3,1},{5,3},{7,5},{8,14},{10,8},{12,... | collective-permute-start | bytes 24584 | tf_op jit(solution)/shard_map/ppermute | solution.py:15
  35.7 2.3 %convert_reduce_fusion = (f32[512]{0:T(512)S(1)}, bf16[1024,512]{0,1:T(8,128)(2,1)S(1)}) fusion(f32[1024]{0:T(1024)S(1)} %bitcast.173, f32[1024]{0:T(1024)S(1)} %fusion.25, f32[1024]{0:T(1024)S(1)} %slice_reduce_fusion, f32[1024,512]{0,1:T(8,128)} %copy-done.1, f32[512]{0:T(512)S(1)} %get-tuple-element.38), kind=kLoop, calls=%fused_computation.8 | loop fusion | flops 3669504 | bytes 3162112 | tf_op jit(solution)/shard_map/reduce_sum | solution.py:68
  45.4 1.9 %collective-permute-done = f32[2,1024]{1,0:T(2,128)S(1)} collective-permute-done((f32[2,1024]{1,0:T(2,128)S(1)}, f32[2,1024]{1,0:T(2,128)S(1)}, u32[]{:S(2)}, u32[]{:S(2)}) %collective-permute-start) | collective-permute-done | bytes 8224 | tf_op jit(solution)/shard_map/ppermute | solution.py:15
  49.6 1.6 %collective-permute-start.28 = (f32[1024]{0:T(1024)S(1)}, f32[1024]{0:T(1024)S(1)}, u32[]{:S(2)}, u32[]{:S(2)}) collective-permute-start(f32[1024]{0:T(1024)S(1)} %add_add_fusion), channel_id=1, source_target_pairs={{0,1},{1,0},{2,3},{3,2},{4,5},{5,4},{6,7},{7,6},{8,9},{9,8},{10,11... | collective-permute-start | bytes 12296 | tf_op jit(solution)/shard_map/ppermute | solution.py:25
  53.2 1.5 %collective-permute-start.27 = (f32[512]{0:T(512)S(1)}, f32[512]{0:T(512)S(1)}, u32[]{:S(2)}, u32[]{:S(2)}) collective-permute-start(f32[512]{0:T(512)S(1)} %add.182), channel_id=1, source_target_pairs={{0,16},{8,24},{16,0},{24,8},{1,17},{9,25},{17,1},{25,9},{2,18},{10... | collective-permute-start | bytes 6152 | tf_op jit(solution)/shard_map/ppermute | solution.py:25
  55.3 1.5 %collective-permute-done.27 = f32[512]{0:T(512)S(1)} collective-permute-done((f32[512]{0:T(512)S(1)}, f32[512]{0:T(512)S(1)}, u32[]{:S(2)}, u32[]{:S(2)}) %collective-permute-start.27) | collective-permute-done | bytes 2080 | tf_op jit(solution)/shard_map/ppermute | solution.py:25
  56.8 1.5 %collective-permute-start.20 = (f32[512]{0:T(512)S(1)}, f32[512]{0:T(512)S(1)}, u32[]{:S(2)}, u32[]{:S(2)}) collective-permute-start(f32[512]{0:T(512)S(1)} %add.176), channel_id=1, source_target_pairs={{0,16},{8,24},{16,0},{24,8},{1,17},{9,25},{17,1},{25,9},{2,18},{10... | collective-permute-start | bytes 6152 | tf_op jit(solution)/shard_map/ppermute | solution.py:25
  58.3 2.1 %collective-permute-done.20 = f32[512]{0:T(512)S(1)} collective-permute-done((f32[512]{0:T(512)S(1)}, f32[512]{0:T(512)S(1)}, u32[]{:S(2)}, u32[]{:S(2)}) %collective-permute-start.20) | collective-permute-done | bytes 2080 | tf_op jit(solution)/shard_map/ppermute | solution.py:25
  60.4 1.5 %collective-permute-start.13 = (f32[512]{0:T(512)S(1)}, f32[512]{0:T(512)S(1)}, u32[]{:S(2)}, u32[]{:S(2)}) collective-permute-start(f32[512]{0:T(512)S(1)} %add.170), channel_id=1, source_target_pairs={{0,16},{8,24},{16,0},{24,8},{1,17},{9,25},{17,1},{25,9},{2,18},{10... | collective-permute-start | bytes 6152 | tf_op jit(solution)/shard_map/ppermute | solution.py:25
  61.9 2.1 %collective-permute-done.13 = f32[512]{0:T(512)S(1)} collective-permute-done((f32[512]{0:T(512)S(1)}, f32[512]{0:T(512)S(1)}, u32[]{:S(2)}, u32[]{:S(2)}) %collective-permute-start.13) | collective-permute-done | bytes 2080 | tf_op jit(solution)/shard_map/ppermute | solution.py:25
  64.0 1.5 %collective-permute-start.6 = (f32[512]{0:T(512)S(1)}, f32[512]{0:T(512)S(1)}, u32[]{:S(2)}, u32[]{:S(2)}) collective-permute-start(f32[512]{0:T(512)S(1)} %add.164), channel_id=1, source_target_pairs={{0,16},{8,24},{16,0},{24,8},{1,17},{9,25},{17,1},{25,9},{2,18},{10... | collective-permute-start | bytes 6152 | tf_op jit(solution)/shard_map/ppermute | solution.py:25
  65.5 2.1 %collective-permute-done.6 = f32[512]{0:T(512)S(1)} collective-permute-done((f32[512]{0:T(512)S(1)}, f32[512]{0:T(512)S(1)}, u32[]{:S(2)}, u32[]{:S(2)}) %collective-permute-start.6) | collective-permute-done | bytes 2080 | tf_op jit(solution)/shard_map/ppermute | solution.py:25
  67.8 1.6 %collective-permute-start.25 = (f32[1,512,256]{2,1,0:T(8,128)S(1)}, f32[1,512,256]{2,1,0:T(8,128)S(1)}, u32[]{:S(2)}, u32[]{:S(2)}) collective-permute-start(f32[1,512,256]{2,1,0:T(8,128)S(1)} %constant_dynamic-slice_fusion), channel_id=1, source_target_pairs={{0,16},{8,24},{16,0},{24,8},{1,17},{9,25},{17,1},{25,9},{2,18},{10... | collective-permute-start | bytes 1572872 | tf_op jit(solution)/shard_map/ppermute | solution.py:40
  70.4 1.6 %collective-permute-start.11 = (f32[1,512,256]{2,1,0:T(8,128)S(1)}, f32[1,512,256]{2,1,0:T(8,128)S(1)}, u32[]{:S(2)}, u32[]{:S(2)}) collective-permute-start(f32[1,512,256]{2,1,0:T(8,128)S(1)} %constant_dynamic-slice_fusion.2), channel_id=1, source_target_pairs={{0,16},{8,24},{16,0},{24,8},{1,17},{9,25},{17,1},{25,9},{2,18},{10... | collective-permute-start | bytes 1572872 | tf_op jit(solution)/shard_map/ppermute | solution.py:40
  72.7 10.0 %collective-permute-done.25 = f32[1,512,256]{2,1,0:T(8,128)S(1)} collective-permute-done((f32[1,512,256]{2,1,0:T(8,128)S(1)}, f32[1,512,256]{2,1,0:T(8,128)S(1)}, u32[]{:S(2)}, u32[]{:S(2)}) %collective-permute-start.25) | collective-permute-done | bytes 524320 | tf_op jit(solution)/shard_map/ppermute | solution.py:40
  83.8 10.1 %collective-permute-done.18 = f32[1,512,256]{2,1,0:T(8,128)S(1)} collective-permute-done((f32[1,512,256]{2,1,0:T(8,128)S(1)}, f32[1,512,256]{2,1,0:T(8,128)S(1)}, u32[]{:S(2)}, u32[]{:S(2)}) %collective-permute-start.18) | collective-permute-done | bytes 524320 | tf_op jit(solution)/shard_map/ppermute | solution.py:40
  95.0 9.5 %collective-permute-done.11 = f32[1,512,256]{2,1,0:T(8,128)S(1)} collective-permute-done((f32[1,512,256]{2,1,0:T(8,128)S(1)}, f32[1,512,256]{2,1,0:T(8,128)S(1)}, u32[]{:S(2)}, u32[]{:S(2)}) %collective-permute-start.11) | collective-permute-done | bytes 524320 | tf_op jit(solution)/shard_map/ppermute | solution.py:40
  105.6 4.5 %collective-permute-done.4 = f32[1,512,256]{2,1,0:T(8,128)S(1)} collective-permute-done((f32[1,512,256]{2,1,0:T(8,128)S(1)}, f32[1,512,256]{2,1,0:T(8,128)S(1)}, u32[]{:S(2)}, u32[]{:S(2)}) %collective-permute-start.4) | collective-permute-done | bytes 524320 | tf_op jit(solution)/shard_map/ppermute | solution.py:40
  (132 shorter events, 30.8 us)
Async XLA Ops:
  7.4 22.6 %collective-permute-start.23 = (f32[2,1024]{1,0:T(2,128)S(1)}, f32[2,1024]{1,0:T(2,128)S(1)}, u32[]{:S(2)}, u32[]{:S(2)}) collective-permute-start(f32[2,1024]{1,0:T(2,128)S(1)} %get-tuple-element.29), channel_id=1, source_target_pairs={{0,6},{2,0},{4,2},{6,4},{1,7},{3,1},{5,3},{7,5},{8,14},{10,8},{12,... | collective-permute-start | bytes 24584 | tf_op jit(solution)/shard_map/ppermute | solution.py:15
  12.6 13.5 %collective-permute-start.22 = (f32[2,1024]{1,0:T(2,128)S(1)}, f32[2,1024]{1,0:T(2,128)S(1)}, u32[]{:S(2)}, u32[]{:S(2)}) collective-permute-start(f32[2,1024]{1,0:T(2,128)S(1)} %get-tuple-element.29), channel_id=1, source_target_pairs={{0,4},{2,6},{4,0},{6,2},{1,5},{3,7},{5,1},{7,3},{8,12},{10,14},{12... | collective-permute-start | bytes 24584 | tf_op jit(solution)/shard_map/ppermute | solution.py:15
  12.6 13.6 %collective-permute-start.21 = (f32[2,1024]{1,0:T(2,128)S(1)}, f32[2,1024]{1,0:T(2,128)S(1)}, u32[]{:S(2)}, u32[]{:S(2)}) collective-permute-start(f32[2,1024]{1,0:T(2,128)S(1)} %get-tuple-element.29), channel_id=1, source_target_pairs={{0,2},{2,4},{4,6},{6,0},{1,3},{3,5},{5,7},{7,1},{8,10},{10,12},{12... | collective-permute-start | bytes 24584 | tf_op jit(solution)/shard_map/ppermute | solution.py:15
  16.7 17.8 %collective-permute-start.16 = (f32[2,1024]{1,0:T(2,128)S(1)}, f32[2,1024]{1,0:T(2,128)S(1)}, u32[]{:S(2)}, u32[]{:S(2)}) collective-permute-start(f32[2,1024]{1,0:T(2,128)S(1)} %get-tuple-element.27), channel_id=1, source_target_pairs={{0,6},{2,0},{4,2},{6,4},{1,7},{3,1},{5,3},{7,5},{8,14},{10,8},{12,... | collective-permute-start | bytes 24584 | tf_op jit(solution)/shard_map/ppermute | solution.py:15
  19.5 10.8 %collective-permute-start.15 = (f32[2,1024]{1,0:T(2,128)S(1)}, f32[2,1024]{1,0:T(2,128)S(1)}, u32[]{:S(2)}, u32[]{:S(2)}) collective-permute-start(f32[2,1024]{1,0:T(2,128)S(1)} %get-tuple-element.27), channel_id=1, source_target_pairs={{0,4},{2,6},{4,0},{6,2},{1,5},{3,7},{5,1},{7,3},{8,12},{10,14},{12... | collective-permute-start | bytes 24584 | tf_op jit(solution)/shard_map/ppermute | solution.py:15
  26.1 5.5 %collective-permute-start.14 = (f32[2,1024]{1,0:T(2,128)S(1)}, f32[2,1024]{1,0:T(2,128)S(1)}, u32[]{:S(2)}, u32[]{:S(2)}) collective-permute-start(f32[2,1024]{1,0:T(2,128)S(1)} %get-tuple-element.27), channel_id=1, source_target_pairs={{0,2},{2,4},{4,6},{6,0},{1,3},{3,5},{5,7},{7,1},{8,10},{10,12},{12... | collective-permute-start | bytes 24584 | tf_op jit(solution)/shard_map/ppermute | solution.py:15
  26.2 15.8 %collective-permute-start.9 = (f32[2,1024]{1,0:T(2,128)S(1)}, f32[2,1024]{1,0:T(2,128)S(1)}, u32[]{:S(2)}, u32[]{:S(2)}) collective-permute-start(f32[2,1024]{1,0:T(2,128)S(1)} %get-tuple-element.25), channel_id=1, source_target_pairs={{0,6},{2,0},{4,2},{6,4},{1,7},{3,1},{5,3},{7,5},{8,14},{10,8},{12,... | collective-permute-start | bytes 24584 | tf_op jit(solution)/shard_map/ppermute | solution.py:15
  30.1 11.7 %collective-permute-start.8 = (f32[2,1024]{1,0:T(2,128)S(1)}, f32[2,1024]{1,0:T(2,128)S(1)}, u32[]{:S(2)}, u32[]{:S(2)}) collective-permute-start(f32[2,1024]{1,0:T(2,128)S(1)} %get-tuple-element.25), channel_id=1, source_target_pairs={{0,4},{2,6},{4,0},{6,2},{1,5},{3,7},{5,1},{7,3},{8,12},{10,14},{12... | collective-permute-start | bytes 24584 | tf_op jit(solution)/shard_map/ppermute | solution.py:15
  30.3 11.6 %collective-permute-start.7 = (f32[2,1024]{1,0:T(2,128)S(1)}, f32[2,1024]{1,0:T(2,128)S(1)}, u32[]{:S(2)}, u32[]{:S(2)}) collective-permute-start(f32[2,1024]{1,0:T(2,128)S(1)} %get-tuple-element.25), channel_id=1, source_target_pairs={{0,2},{2,4},{4,6},{6,0},{1,3},{3,5},{5,7},{7,1},{8,10},{10,12},{12... | collective-permute-start | bytes 24584 | tf_op jit(solution)/shard_map/ppermute | solution.py:15
  31.6 15.7 %collective-permute-start.2 = (f32[2,1024]{1,0:T(2,128)S(1)}, f32[2,1024]{1,0:T(2,128)S(1)}, u32[]{:S(2)}, u32[]{:S(2)}) collective-permute-start(f32[2,1024]{1,0:T(2,128)S(1)} %get-tuple-element.23), channel_id=1, source_target_pairs={{0,6},{2,0},{4,2},{6,4},{1,7},{3,1},{5,3},{7,5},{8,14},{10,8},{12,... | collective-permute-start | bytes 24584 | tf_op jit(solution)/shard_map/ppermute | solution.py:15
  34.4 10.9 %collective-permute-start.1 = (f32[2,1024]{1,0:T(2,128)S(1)}, f32[2,1024]{1,0:T(2,128)S(1)}, u32[]{:S(2)}, u32[]{:S(2)}) collective-permute-start(f32[2,1024]{1,0:T(2,128)S(1)} %get-tuple-element.23), channel_id=1, source_target_pairs={{0,4},{2,6},{4,0},{6,2},{1,5},{3,7},{5,1},{7,3},{8,12},{10,14},{12... | collective-permute-start | bytes 24584 | tf_op jit(solution)/shard_map/ppermute | solution.py:15
  41.8 5.5 %collective-permute-start = (f32[2,1024]{1,0:T(2,128)S(1)}, f32[2,1024]{1,0:T(2,128)S(1)}, u32[]{:S(2)}, u32[]{:S(2)}) collective-permute-start(f32[2,1024]{1,0:T(2,128)S(1)} %get-tuple-element.23), channel_id=1, source_target_pairs={{0,2},{2,4},{4,6},{6,0},{1,3},{3,5},{5,7},{7,1},{8,10},{10,12},{12... | collective-permute-start | bytes 24584 | tf_op jit(solution)/shard_map/ppermute | solution.py:15
  41.9 9.3 %collective-permute-start.26 = (f32[512]{0:T(512)S(1)}, f32[512]{0:T(512)S(1)}, u32[]{:S(2)}, u32[]{:S(2)}) collective-permute-start(f32[512]{0:T(512)S(1)} %get-tuple-element.12), channel_id=1, source_target_pairs={{0,8},{8,0},{16,24},{24,16},{1,9},{9,1},{17,25},{25,17},{2,10},{10... | collective-permute-start | bytes 6152 | tf_op jit(solution)/shard_map/ppermute | solution.py:25
  42.0 9.4 %collective-permute-start.19 = (f32[512]{0:T(512)S(1)}, f32[512]{0:T(512)S(1)}, u32[]{:S(2)}, u32[]{:S(2)}) collective-permute-start(f32[512]{0:T(512)S(1)} %get-tuple-element.10), channel_id=1, source_target_pairs={{0,8},{8,0},{16,24},{24,16},{1,9},{9,1},{17,25},{25,17},{2,10},{10... | collective-permute-start | bytes 6152 | tf_op jit(solution)/shard_map/ppermute | solution.py:25
  45.3 6.5 %collective-permute-start.12 = (f32[512]{0:T(512)S(1)}, f32[512]{0:T(512)S(1)}, u32[]{:S(2)}, u32[]{:S(2)}) collective-permute-start(f32[512]{0:T(512)S(1)} %get-tuple-element.8), channel_id=1, source_target_pairs={{0,8},{8,0},{16,24},{24,16},{1,9},{9,1},{17,25},{25,17},{2,10},{10... | collective-permute-start | bytes 6152 | tf_op jit(solution)/shard_map/ppermute | solution.py:25
  49.6 3.7 %collective-permute-start.28 = (f32[1024]{0:T(1024)S(1)}, f32[1024]{0:T(1024)S(1)}, u32[]{:S(2)}, u32[]{:S(2)}) collective-permute-start(f32[1024]{0:T(1024)S(1)} %add_add_fusion), channel_id=1, source_target_pairs={{0,1},{1,0},{2,3},{3,2},{4,5},{5,4},{6,7},{7,6},{8,9},{9,8},{10,11... | collective-permute-start | bytes 12296 | tf_op jit(solution)/shard_map/ppermute | solution.py:25
  51.2 16.4 %collective-permute-start.24 = (f32[2,512,256]{2,1,0:T(8,128)S(1)}, f32[2,512,256]{2,1,0:T(8,128)S(1)}, u32[]{:S(2)}, u32[]{:S(2)}) collective-permute-start(f32[2,512,256]{2,1,0:T(8,128)S(1)} %dynamic-slice_bitcast_fusion), channel_id=1, source_target_pairs={{0,8},{8,0},{16,24},{24,16},{1,9},{9,1},{17,25},{25,17},{2,10},{10... | collective-permute-start | bytes 3145736 | tf_op jit(solution)/shard_map/ppermute | solution.py:40
  51.5 17.9 %collective-permute-start.17 = (f32[2,512,256]{2,1,0:T(8,128)S(1)}, f32[2,512,256]{2,1,0:T(8,128)S(1)}, u32[]{:S(2)}, u32[]{:S(2)}) collective-permute-start(f32[2,512,256]{2,1,0:T(8,128)S(1)} %dynamic-slice_bitcast_fusion.1), channel_id=1, source_target_pairs={{0,8},{8,0},{16,24},{24,16},{1,9},{9,1},{17,25},{25,17},{2,10},{10... | collective-permute-start | bytes 3145736 | tf_op jit(solution)/shard_map/ppermute | solution.py:40
  51.8 18.3 %collective-permute-start.10 = (f32[2,512,256]{2,1,0:T(8,128)S(1)}, f32[2,512,256]{2,1,0:T(8,128)S(1)}, u32[]{:S(2)}, u32[]{:S(2)}) collective-permute-start(f32[2,512,256]{2,1,0:T(8,128)S(1)} %dynamic-slice_bitcast_fusion.2), channel_id=1, source_target_pairs={{0,8},{8,0},{16,24},{24,16},{1,9},{9,1},{17,25},{25,17},{2,10},{10... | collective-permute-start | bytes 3145736 | tf_op jit(solution)/shard_map/ppermute | solution.py:40
  52.0 19.9 %collective-permute-start.3 = (f32[2,512,256]{2,1,0:T(8,128)S(1)}, f32[2,512,256]{2,1,0:T(8,128)S(1)}, u32[]{:S(2)}, u32[]{:S(2)}) collective-permute-start(f32[2,512,256]{2,1,0:T(8,128)S(1)} %dynamic-slice_bitcast_fusion.3), channel_id=1, source_target_pairs={{0,8},{8,0},{16,24},{24,16},{1,9},{9,1},{17,25},{25,17},{2,10},{10... | collective-permute-start | bytes 3145736 | tf_op jit(solution)/shard_map/ppermute | solution.py:40
  67.8 14.9 %collective-permute-start.25 = (f32[1,512,256]{2,1,0:T(8,128)S(1)}, f32[1,512,256]{2,1,0:T(8,128)S(1)}, u32[]{:S(2)}, u32[]{:S(2)}) collective-permute-start(f32[1,512,256]{2,1,0:T(8,128)S(1)} %constant_dynamic-slice_fusion), channel_id=1, source_target_pairs={{0,16},{8,24},{16,0},{24,8},{1,17},{9,25},{17,1},{25,9},{2,18},{10... | collective-permute-start | bytes 1572872 | tf_op jit(solution)/shard_map/ppermute | solution.py:40
  69.6 24.3 %collective-permute-start.18 = (f32[1,512,256]{2,1,0:T(8,128)S(1)}, f32[1,512,256]{2,1,0:T(8,128)S(1)}, u32[]{:S(2)}, u32[]{:S(2)}) collective-permute-start(f32[1,512,256]{2,1,0:T(8,128)S(1)} %constant_dynamic-slice_fusion.1), channel_id=1, source_target_pairs={{0,16},{8,24},{16,0},{24,8},{1,17},{9,25},{17,1},{25,9},{2,18},{10... | collective-permute-start | bytes 1572872 | tf_op jit(solution)/shard_map/ppermute | solution.py:40
  70.4 34.1 %collective-permute-start.11 = (f32[1,512,256]{2,1,0:T(8,128)S(1)}, f32[1,512,256]{2,1,0:T(8,128)S(1)}, u32[]{:S(2)}, u32[]{:S(2)}) collective-permute-start(f32[1,512,256]{2,1,0:T(8,128)S(1)} %constant_dynamic-slice_fusion.2), channel_id=1, source_target_pairs={{0,16},{8,24},{16,0},{24,8},{1,17},{9,25},{17,1},{25,9},{2,18},{10... | collective-permute-start | bytes 1572872 | tf_op jit(solution)/shard_map/ppermute | solution.py:40
  72.1 38.0 %collective-permute-start.4 = (f32[1,512,256]{2,1,0:T(8,128)S(1)}, f32[1,512,256]{2,1,0:T(8,128)S(1)}, u32[]{:S(2)}, u32[]{:S(2)}) collective-permute-start(f32[1,512,256]{2,1,0:T(8,128)S(1)} %constant_dynamic-slice_fusion.3), channel_id=1, source_target_pairs={{0,16},{8,24},{16,0},{24,8},{1,17},{9,25},{17,1},{25,9},{2,18},{10... | collective-permute-start | bytes 1572872 | tf_op jit(solution)/shard_map/ppermute | solution.py:40
  (14 other events, 58.3 us)
